TPU v7x, 128 devices: a whole 4x4x4 slice. The times are simulated.
128 devices in a mesh: expert: 32 (over y, z, core), dp: 4 (over x).
Axes of the slice: x: 4, y: 4, z: 4, core: 2. Of those that a mesh axis runs over, the one named last changes fastest.
Arguments:
- activations: bfloat16 [2048, 7168], P(('expert', 'dp')), may hold values from -6 to 6
- cotangent: bfloat16 [2048, 7168], P(('expert', 'dp')), may hold values from -6 to 6
- route_ids: int32 [2048, 8], P(('expert', 'dp')), may hold values from 0 to 31, all different within a row; in each aligned block of 16 rows (0 to 15, 16 to 31, ...) at most 5 rows name the same one
- route_weights: float32 [2048, 8], P(('expert', 'dp')), may hold values from 0.05 to 0.6
- gate_weights: bfloat16 [32, 7168, 1024], P('expert', 'dp'), may hold values from -0.0625 to 0.0625
- up_weights: bfloat16 [32, 7168, 1024], P('expert', 'dp'), may hold values from -0.0625 to 0.0625
- down_weights: bfloat16 [32, 1024, 7168], P('expert', None, 'dp'), may hold values from -0.1875 to 0.1875
Outputs:
- grad_input: bfloat16 [2048, 7168], P(('expert', 'dp'))
- grad_gate: bfloat16 [32, 7168, 1024], P('expert', 'dp')
- grad_up: bfloat16 [32, 7168, 1024], P('expert', 'dp')
- grad_down: bfloat16 [32, 1024, 7168], P('expert', None, 'dp')
Inputs may be any that keep to these rules, and one draw needn't show every extreme that they name: `route_ids`: each token names 8 different experts. Among the routes of one device's 16 tokens, no expert is named more than 5 times, a bound that some block reaches.
All inputs are finite; a program needn't handle non-finite values.
Results may differ from a plain program's by a relative error of at most 0.0064.
Values may be sent and summed in bfloat16 or wider, within the bound.
No kernel may reach another device: no remote copies, remote signals or barrier semaphores. Data moves between devices by JAX's collectives and lax.ppermute only.
A program may use at most 128 MiB of HBM per device.

v0:
```python
import jax
import jax.numpy as jnp
from jax import lax
from jax.sharding import PartitionSpec as P


def swiglu_back(gate, upper, upstream):
    sigma = jax.nn.sigmoid(gate)
    silu_gate = gate * sigma
    activated = (silu_gate * upper).astype(jnp.bfloat16)
    grad_pre = (upstream * upper * sigma * (1.0 + gate * (1.0 - sigma))).astype(jnp.bfloat16)
    grad_lin = (upstream * silu_gate).astype(jnp.bfloat16)
    return (grad_pre, grad_lin, activated)


def contract_rows(left, right):
    return lax.dot_general(
        left, right, (((0,), (0,)), ((), ())), preferred_element_type=jnp.float32
    )


def shards(
    activations, cotangent, route_ids, route_weights, gate_weights, up_weights, down_weights
):
    tok_rows, width = activations.shape
    topk = route_ids.shape[1]
    num_dp = lax.axis_size("dp")
    num_exp = lax.axis_size("expert")
    slice_width = gate_weights.shape[1]
    hidden = gate_weights.shape[2]
    capacity = min(tok_rows, 5 * tok_rows * topk // (4 * num_exp))
    buffer_rows = num_exp * num_dp * capacity
    flat_ids = route_ids.reshape(-1)
    expert_iota = jnp.arange(num_exp, dtype=jnp.int32)
    onehot = (flat_ids[:, None] == expert_iota[None, :]).astype(jnp.int32)
    before = jnp.cumsum(onehot, axis=0) - onehot
    slot = jnp.sum(before * onehot, axis=1)
    target = (flat_ids * capacity + slot).reshape(tok_rows, topk)
    slot_iota = jnp.arange(num_exp * capacity, dtype=jnp.int32)
    matches = target[:, :, None] == slot_iota[None, None, :]
    placing = jnp.any(matches, axis=1).astype(jnp.bfloat16)
    slot_weight = jnp.sum(jnp.where(matches, route_weights[:, :, None], 0.0), axis=(0, 1))
    send_act = contract_rows(placing, activations).astype(jnp.bfloat16)
    send_cot = (contract_rows(placing, cotangent) * slot_weight[:, None]).astype(jnp.bfloat16)
    send_act = send_act.reshape(num_exp, capacity, num_dp, slice_width)
    send_cot = send_cot.reshape(num_exp, capacity, num_dp, slice_width)
    flat_act = jnp.swapaxes(send_act, 1, 2).reshape(num_exp * num_dp, capacity, slice_width)
    flat_cot = jnp.swapaxes(send_cot, 1, 2).reshape(num_exp * num_dp, capacity, slice_width)
    recv_act, recv_cot = (
        lax.all_to_all(flat_act, ("expert", "dp"), split_axis=0, concat_axis=0, tiled=True),
        lax.all_to_all(flat_cot, ("expert", "dp"), split_axis=0, concat_axis=0, tiled=True),
    )
    recv_act = recv_act.reshape(buffer_rows, slice_width)
    recv_cot = recv_cot.reshape(buffer_rows, slice_width)
    gate_local = gate_weights[0]
    up_local = up_weights[0]
    down_local = down_weights[0]
    act_rows = recv_act
    cot_rows = recv_cot
    gate_part = jnp.dot(act_rows, gate_local, preferred_element_type=jnp.float32)
    up_part = jnp.dot(act_rows, up_local, preferred_element_type=jnp.float32)
    back_part = lax.dot_general(
        cot_rows, down_local, (((1,), (1,)), ((), ())), preferred_element_type=jnp.float32
    )
    summed = lax.psum(jnp.concatenate([gate_part, up_part, back_part], axis=1), "dp")
    grad_pre, grad_lin, activated = swiglu_back(
        summed[:, :hidden], summed[:, hidden : 2 * hidden], summed[:, 2 * hidden :]
    )
    act_rows = recv_act
    cot_rows = recv_cot
    rows_back = lax.dot_general(
        grad_pre, gate_local, (((1,), (1,)), ((), ())), preferred_element_type=jnp.float32
    ) + lax.dot_general(
        grad_lin, up_local, (((1,), (1,)), ((), ())), preferred_element_type=jnp.float32
    )
    grad_gate = contract_rows(act_rows, grad_pre).astype(jnp.bfloat16)[None]
    grad_up = contract_rows(act_rows, grad_lin).astype(jnp.bfloat16)[None]
    grad_down = contract_rows(activated, cot_rows).astype(jnp.bfloat16)[None]
    back_rows = rows_back.astype(jnp.bfloat16)
    flat_back = back_rows.reshape(num_exp * num_dp, capacity, slice_width)
    arrived = lax.all_to_all(flat_back, ("expert", "dp"), split_axis=0, concat_axis=0, tiled=True)
    arrived = jnp.swapaxes(arrived.reshape(num_exp, num_dp, capacity, slice_width), 1, 2)
    arrived = arrived.reshape(num_exp * capacity, width)
    grad_input = jnp.dot(placing, arrived, preferred_element_type=jnp.float32).astype(jnp.bfloat16)
    return (grad_input, grad_gate, grad_up, grad_down)


def solution(mesh):
    placed = (
        P(("expert", "dp"), None),
        P(("expert", "dp"), None),
        P(("expert", "dp"), None),
        P(("expert", "dp"), None),
        P("expert", "dp", None),
        P("expert", "dp", None),
        P("expert", None, "dp"),
    )
    return jax.shard_map(
        shards,
        mesh=mesh,
        in_specs=placed,
        out_specs=(
            P(("expert", "dp"), None),
            P("expert", "dp", None),
            P("expert", "dp", None),
            P("expert", None, "dp"),
        ),
        check_vma=False,
    )
```

profile of v0, /device:TPU:1, one launch (start us, length us, event | category | flops | bytes accessed | tf_op | source)
XLA Modules:
  0.0 371.8 jit_solution(10881495854793656829)
XLA Ops:
  7.2 0.0 copy-start
  7.2 0.8 copy.30
  8.0 0.1 eq.28
  8.1 0.1 fusion.19
  8.2 0.2 reduce_window_sum.11
  8.3 0.2 select_reduce_fusion.1
  8.5 0.1 reduce_sum.21
  8.6 0.1 fusion.18
  8.8 2.2 convolution_convert_fusion
  10.9 3.5 reshape.45
  14.4 2.5 copy.38
  16.9 11.9 %all-to-all-start = ((bf16[128,5,1792]{2,1,0:T(8,128)(2,1)}), bf16[128,5,1792]{2,1,0:T(8,128)(2,1)}, u32[]{:S(2)}, u32[]{:S(2)}) async-start(bf16[128,5,1792]{2,1,0:T(8,128)(2,1)} %bitcast.49), calls=%async_computation | async-start | bytes 7340032 | tf_op jit(solution)/shard_map/all_to_all | solution.py:50
  28.8 0.1 copy.34
  28.9 0.1 select_reduce_fusion
  29.0 0.8 fusion
  29.8 2.9 reshape.48
  32.8 4.2 %copy.39 = bf16[32,4,5,1792]{3,2,1,0:T(8,128)(2,1)} copy(bf16[32,4,5,1792]{3,1,2,0:T(4,128)(2,1)} %bitcast.52) | data formatting | bytes 4587520 | tf_op jit(solution)/shard_map/reshape | solution.py:48
  36.9 39.4 %all-to-all-done = bf16[128,5,1792]{2,1,0:T(8,128)(2,1)} async-done(((bf16[128,5,1792]{2,1,0:T(8,128)(2,1)}), bf16[128,5,1792]{2,1,0:T(8,128)(2,1)}, u32[]{:S(2)}, u32[]{:S(2)}) %all-to-all-start) | async-done | bytes 2293792 | tf_op jit(solution)/shard_map/all_to_all | solution.py:50
  76.4 4.7 %all-to-all-start.1 = ((bf16[128,5,1792]{2,1,0:T(8,128)(2,1)}), bf16[128,5,1792]{2,1,0:T(8,128)(2,1)}, u32[]{:S(2)}, u32[]{:S(2)}) async-start(bf16[128,5,1792]{2,1,0:T(8,128)(2,1)} %bitcast.48), calls=%async_computation.1 | async-start | bytes 7340032 | tf_op jit(solution)/shard_map/all_to_all | solution.py:51
  81.1 0.2 all-reduce.2.cloned.1.call-start
  81.3 5.4 %reshape.47 = bf16[640,1792]{1,0:T(8,128)(2,1)} reshape(bf16[128,5,1792]{2,1,0:T(8,128)(2,1)} %all-to-all-done) | data formatting | bytes 4587520 | tf_op jit(solution)/shard_map/reshape | solution.py:53
  86.7 5.4 %fusion.5 = f32[640,1024]{1,0:T(8,128)S(1)} fusion(bf16[640,1792]{1,0:T(8,128)(2,1)} %reshape.47, bf16[1,1792,1024]{2,1,0:T(8,128)(2,1)} %param.12), kind=kOutput, calls=%fused_computation.13 | convolution fusion | flops 2348810240 | bytes 8585216 | tf_op jit(solution)/shard_map/dot_general | solution.py:61
  92.1 4.0 %fusion.9 = f32[640,1024]{1,0:T(8,128)} fusion(bf16[640,1792]{1,0:T(8,128)(2,1)S(1)} %copy-done.3, bf16[1,1792,1024]{2,1,0:T(8,128)(2,1)S(1)} %copy-done.12), kind=kOutput, calls=%fused_computation.17 | convolution fusion | flops 2348810240 | bytes 8585216 | tf_op jit(solution)/shard_map/dot_general | solution.py:60
  96.1 32.5 %all-to-all-done.1 = bf16[128,5,1792]{2,1,0:T(8,128)(2,1)} async-done(((bf16[128,5,1792]{2,1,0:T(8,128)(2,1)}), bf16[128,5,1792]{2,1,0:T(8,128)(2,1)}, u32[]{:S(2)}, u32[]{:S(2)}) %all-to-all-start.1) | async-done | bytes 2293792 | tf_op jit(solution)/shard_map/all_to_all | solution.py:51
  128.6 5.4 %reshape.50 = bf16[640,1792]{1,0:T(8,128)(2,1)} reshape(bf16[128,5,1792]{2,1,0:T(8,128)(2,1)} %all-to-all-done.1) | data formatting | bytes 4587520 | tf_op jit(solution)/shard_map/reshape | solution.py:54
  134.0 5.4 %fusion.1 = f32[640,1024]{1,0:T(8,128)S(1)} fusion(bf16[640,1792]{1,0:T(8,128)(2,1)} %reshape.50, bf16[1,1024,1792]{2,1,0:T(8,128)(2,1)} %param.13), kind=kOutput, calls=%fused_computation.9 | convolution fusion | flops 2348810240 | bytes 8585216 | tf_op jit(solution)/shard_map/dot_general | solution.py:62
  139.5 3.5 pad_maximum_fusion
  142.9 0.0 all-reduce.2.cloned.1.call-update
  142.9 147.8 %all-reduce.2.cloned.1.call-done = f32[640,3072]{1,0:T(8,128)} async-done(((f32[640,3072]{1,0:T(8,128)}), f32[640,3072]{1,0:T(8,128)}) %all-reduce.2.cloned.1.call-update) | async-done | bytes 7864336 | tf_op jit(solution)/shard_map/psum | solution.py:65
  290.7 5.0 %multiply_convert_fusion.2 = (bf16[640,1024]{1,0:T(8,128)(2,1)S(1)}, bf16[640,1024]{1,0:T(8,128)(2,1)S(1)}) fusion(f32[640,3072]{1,0:T(8,128)} %all-reduce.2.cloned.1.call-done), kind=kLoop, calls=%fused_computation.24 | loop fusion | flops 8519680 | bytes 10485760 | tf_op jit(solution)/shard_map/convert_element_type | solution.py:11
  295.7 0.0 copy-start.8
  295.8 0.0 copy-done.11
  295.8 0.0 copy-start.13
  295.8 2.6 fusion.3
  298.4 0.3 copy-done.13
  298.7 2.6 add_convert_fusion
  301.3 2.7 reshape.51
  304.1 8.9 %all-to-all-start.2 = ((bf16[128,5,1792]{2,1,0:T(8,128)(2,1)}), bf16[128,5,1792]{2,1,0:T(8,128)(2,1)}, u32[]{:S(2)}, u32[]{:S(2)}) async-start(bf16[128,5,1792]{2,1,0:T(8,128)(2,1)} %reshape.51), calls=%async_computation.2 | async-start | bytes 7340032 | tf_op jit(solution)/shard_map/all_to_all | solution.py:81
  313.0 5.9 %fusion.11 = bf16[1,1792,1024]{2,1,0:T(8,128)(2,1)} fusion(bf16[640,1792]{1,0:T(8,128)(2,1)S(1)} %copy-done.4, bf16[640,1024]{1,0:T(8,128)(2,1)} %copy-done.8), kind=kOutput, calls=%fused_computation.19 | convolution fusion | flops 2350645248 | bytes 7274496 | tf_op jit(solution)/shard_map/dot_general | solution.py:17
  318.9 0.0 copy-done.7
  318.9 4.5 %fusion.12 = bf16[1,1792,1024]{2,1,0:T(8,128)(2,1)} fusion(bf16[640,1792]{1,0:T(8,128)(2,1)S(1)} %copy-done.4, bf16[640,1024]{1,0:T(8,128)(2,1)S(1)} %copy-done.7), kind=kOutput, calls=%fused_computation.20 | convolution fusion | flops 2350645248 | bytes 7274496 | tf_op jit(solution)/shard_map/dot_general | solution.py:17
  323.5 0.0 copy-done.5
  323.5 7.6 %fusion.13 = bf16[1,1024,1792]{2,1,0:T(8,128)(2,1)} fusion(bf16[640,1792]{1,0:T(8,128)(2,1)S(1)} %copy-done.5, f32[640,3072]{1,0:T(8,128)} %all-reduce.2.cloned.1.call-done), kind=kOutput, calls=%fused_computation.21 | convolution fusion | flops 2354577408 | bytes 11206656 | tf_op jit(solution)/shard_map/dot_general | solution.py:17
  331.1 29.4 %all-to-all-done.2 = bf16[128,5,1792]{2,1,0:T(8,128)(2,1)} async-done(((bf16[128,5,1792]{2,1,0:T(8,128)(2,1)}), bf16[128,5,1792]{2,1,0:T(8,128)(2,1)}, u32[]{:S(2)}, u32[]{:S(2)}) %all-to-all-start.2) | async-done | bytes 2293792 | tf_op jit(solution)/shard_map/all_to_all | solution.py:81
  360.5 3.0 copy.37
  363.5 0.0 copy-start.1
  363.5 0.3 copy.42
  363.8 1.1 convolution_convert_fusion.1
  (21 shorter events, 0.1 us)
Async XLA Ops:
  7.2 1.6 copy-start
  16.9 11.9 %copy-start.10 = (f32[16,8]{0,1:T(8,128)S(1)}, f32[16,8]{0,1:T(8,128)}, u32[]{:S(2)}) copy-start(f32[16,8]{0,1:T(8,128)} %param.10) | copy-start | bytes 1540
  16.9 12.1 %copy-start.9 = (bf16[16,7168]{1,0:T(8,128)(2,1)S(1)}, bf16[16,7168]{1,0:T(8,128)(2,1)}, u32[]{:S(2)}) copy-start(bf16[16,7168]{1,0:T(8,128)(2,1)} %param.8) | copy-start | bytes 688132
  16.9 59.4 %all-to-all-start = ((bf16[128,5,1792]{2,1,0:T(8,128)(2,1)}), bf16[128,5,1792]{2,1,0:T(8,128)(2,1)}, u32[]{:S(2)}, u32[]{:S(2)}) async-start(bf16[128,5,1792]{2,1,0:T(8,128)(2,1)} %bitcast.49), calls=%async_computation | async-start | bytes 7340032 | tf_op jit(solution)/shard_map/all_to_all | solution.py:50
  76.4 52.3 %all-to-all-start.1 = ((bf16[128,5,1792]{2,1,0:T(8,128)(2,1)}), bf16[128,5,1792]{2,1,0:T(8,128)(2,1)}, u32[]{:S(2)}, u32[]{:S(2)}) async-start(bf16[128,5,1792]{2,1,0:T(8,128)(2,1)} %bitcast.48), calls=%async_computation.1 | async-start | bytes 7340032 | tf_op jit(solution)/shard_map/all_to_all | solution.py:51
  81.1 209.7 %all-reduce.2.cloned.1.call-start = ((), (), s32[]{:S(2)}) async-start(), calls=%async_computation.3 | async-start | bytes 15728640 | tf_op jit(solution)/shard_map/psum | solution.py:65
  86.7 5.4 %copy-start.3 = (bf16[640,1792]{1,0:T(8,128)(2,1)S(1)}, bf16[640,1792]{1,0:T(8,128)(2,1)}, u32[]{:S(2)}) copy-start(bf16[640,1792]{1,0:T(8,128)(2,1)} %reshape.47) | copy-start | bytes 6881284
  86.7 5.4 %copy-start.12 = (bf16[1,1792,1024]{2,1,0:T(8,128)(2,1)S(1)}, bf16[1,1792,1024]{2,1,0:T(8,128)(2,1)}, u32[]{:S(2)}) copy-start(bf16[1,1792,1024]{2,1,0:T(8,128)(2,1)} %param.11) | copy-start | bytes 11010052
  134.0 5.4 %copy-start.2 = (f32[640,1024]{1,0:T(8,128)S(1)}, f32[640,1024]{1,0:T(8,128)}, u32[]{:S(2)}) copy-start(f32[640,1024]{1,0:T(8,128)} %fusion.9) | copy-start | bytes 7864324
  290.7 5.1 %copy-start.11 = (bf16[1,1792,1024]{2,1,0:T(8,128)(2,1)S(1)}, bf16[1,1792,1024]{2,1,0:T(8,128)(2,1)}, u32[]{:S(2)}) copy-start(bf16[1,1792,1024]{2,1,0:T(8,128)(2,1)} %param.12) | copy-start | bytes 11010052
  295.7 2.6 copy-start.6
  295.7 2.6 copy-start.8
  295.8 3.0 copy-start.13
  304.1 8.9 %copy-start.4 = (bf16[640,1792]{1,0:T(8,128)(2,1)S(1)}, bf16[640,1792]{1,0:T(8,128)(2,1)}, u32[]{:S(2)}) copy-start(bf16[640,1792]{1,0:T(8,128)(2,1)} %reshape.47) | copy-start | bytes 6881284
  304.1 56.4 %all-to-all-start.2 = ((bf16[128,5,1792]{2,1,0:T(8,128)(2,1)}), bf16[128,5,1792]{2,1,0:T(8,128)(2,1)}, u32[]{:S(2)}, u32[]{:S(2)}) async-start(bf16[128,5,1792]{2,1,0:T(8,128)(2,1)} %reshape.51), calls=%async_computation.2 | async-start | bytes 7340032 | tf_op jit(solution)/shard_map/all_to_all | solution.py:81
  313.0 6.0 %copy-start.7 = (bf16[640,1024]{1,0:T(8,128)(2,1)S(1)}, bf16[640,1024]{1,0:T(8,128)(2,1)}, u32[]{:S(2)}) copy-start(bf16[640,1024]{1,0:T(8,128)(2,1)} %copy-done.6) | copy-start | bytes 3932164
  318.9 4.5 %copy-start.5 = (bf16[640,1792]{1,0:T(8,128)(2,1)S(1)}, bf16[640,1792]{1,0:T(8,128)(2,1)}, u32[]{:S(2)}) copy-start(bf16[640,1792]{1,0:T(8,128)(2,1)} %reshape.50) | copy-start | bytes 6881284
  363.5 1.4 copy-start.1
Sparse Core Ops, SparseCore 0:
  143.1 147.5 all-reduce.1
where the time goes:
time: 373 us; the launch traced here: 372 us
  waiting for transfers between devices  249 us (67%)
  matrix products  42.2 us (11%)
  local copies, waits for them, and re-layouts  31.3 us (8%)
  starting transfers between devices  25.7 us (7%)
  between operations  14.3 us (4%)
  other arithmetic  9.16 us (2%)
    psum x1, waiting for transfers between devices, shards(): lax.psum(jnp.concatenate([gate_part, up_part, back_part], axis=1), 'dp')  148 us
    all_to_all x1, waiting for transfers between devices, shards(): lax.all_to_all(flat_act, ('expert', 'dp'), split_axis=0, concat_axis=0, t...  39.4 us
    all_to_all x1, waiting for transfers between devices, shards(): lax.all_to_all(flat_cot, ('expert', 'dp'), split_axis=0, concat_axis=0, t...  32.5 us
    all_to_all x1, waiting for transfers between devices, shards(): lax.all_to_all(flat_back, ('expert', 'dp'), split_axis=0, concat_axis=0,...  29.4 us
    dot_general x5, matrix products, contract_rows(): lax.dot_general(left, right, (((0,), (0,)), ((), ())), preferred_element_...  21.1 us
    all_to_all x1, starting transfers between devices, shards(): lax.all_to_all(flat_act, ('expert', 'dp'), split_axis=0, concat_axis=0, t...  11.9 us
    all_to_all x1, starting transfers between devices, shards(): lax.all_to_all(flat_back, ('expert', 'dp'), split_axis=0, concat_axis=0,...  8.88 us
  transfers between devices with their start and end apart: 4, of which 4 were waited for; matrix products, arithmetic and copies ran while one was open for 11% of the time, Pallas kernels for 0%

commit v1 on v0

--- a/solution.py
+++ b/solution.py
@@ -44,30 +44,37 @@
     send_cot = (contract_rows(placing, cotangent) * slot_weight[:, None]).astype(jnp.bfloat16)
     send_act = send_act.reshape(num_exp, capacity, num_dp, slice_width)
     send_cot = send_cot.reshape(num_exp, capacity, num_dp, slice_width)
-    flat_act = jnp.swapaxes(send_act, 1, 2).reshape(num_exp * num_dp, capacity, slice_width)
-    flat_cot = jnp.swapaxes(send_cot, 1, 2).reshape(num_exp * num_dp, capacity, slice_width)
-    recv_act, recv_cot = (
-        lax.all_to_all(flat_act, ("expert", "dp"), split_axis=0, concat_axis=0, tiled=True),
-        lax.all_to_all(flat_cot, ("expert", "dp"), split_axis=0, concat_axis=0, tiled=True),
+    send_both = jnp.concatenate([send_act, send_cot], axis=3)
+    flat_both = jnp.swapaxes(send_both, 1, 2).reshape(
+        num_exp * num_dp, capacity, 2 * slice_width
     )
-    recv_act = recv_act.reshape(buffer_rows, slice_width)
-    recv_cot = recv_cot.reshape(buffer_rows, slice_width)
+    recv_both = lax.all_to_all(flat_both, ("expert", "dp"), split_axis=0, concat_axis=0, tiled=True)
+    recv_both = recv_both.reshape(buffer_rows, 2 * slice_width)
+    act_rows = recv_both[:, :slice_width]
+    cot_rows = recv_both[:, slice_width:]
     gate_local = gate_weights[0]
     up_local = up_weights[0]
     down_local = down_weights[0]
-    act_rows = recv_act
-    cot_rows = recv_cot
     gate_part = jnp.dot(act_rows, gate_local, preferred_element_type=jnp.float32)
     up_part = jnp.dot(act_rows, up_local, preferred_element_type=jnp.float32)
     back_part = lax.dot_general(
         cot_rows, down_local, (((1,), (1,)), ((), ())), preferred_element_type=jnp.float32
     )
-    summed = lax.psum(jnp.concatenate([gate_part, up_part, back_part], axis=1), "dp")
+    summed = lax.psum_scatter(
+        jnp.concatenate([gate_part, up_part, back_part], axis=1),
+        "dp",
+        scatter_dimension=0,
+        tiled=True,
+    )
     grad_pre, grad_lin, activated = swiglu_back(
         summed[:, :hidden], summed[:, hidden : 2 * hidden], summed[:, 2 * hidden :]
     )
-    act_rows = recv_act
-    cot_rows = recv_cot
+    gathered = lax.all_gather(
+        jnp.concatenate([grad_pre, grad_lin, activated], axis=1), "dp", axis=0, tiled=True
+    )
+    grad_pre = gathered[:, :hidden]
+    grad_lin = gathered[:, hidden : 2 * hidden]
+    activated = gathered[:, 2 * hidden :]
     rows_back = lax.dot_general(
         grad_pre, gate_local, (((1,), (1,)), ((), ())), preferred_element_type=jnp.float32
     ) + lax.dot_general(

time: 373 us -> 349 us (0.936)
  waiting for transfers between devices: 249 us -> 150 us
  blocking collectives: 0 us -> 98.5 us
  starting transfers between devices: 25.7 us -> 9.26 us
  local copies, waits for them, and re-layouts: 31.3 us -> 25.7 us
    psum x1 -> x0, waiting for transfers between devices: 148 us -> none  [shards(): lax.psum(jnp.concatenate([gate_part, up_part, back_part], axis=1), 'dp')]
    all_to_all x0 -> x1, blocking collectives: none -> 98.5 us  [shards(): lax.all_to_all(flat_both, ('expert', 'dp'), split_axis=0, concat_axis=0,...]
    reduce_scatter x0 -> x1, waiting for transfers between devices: none -> 72.4 us  [shards(): lax.psum_scatter(jnp.concatenate([gate_part, up_part, back_part], axis=1)...]
    all_to_all x2 -> x0, waiting for transfers between devices: 71.9 us -> none  [the longest x1 39.4 us: shards(): lax.all_to_all(flat_act, ('expert', 'dp'), split_axis=0, concat_axis=0, t...]
    all_gather x0 -> x1, waiting for transfers between devices: none -> 45.8 us  [shards(): lax.all_gather(jnp.concatenate([grad_pre, grad_lin, activated], axis=1),...]
    all_to_all x2 -> x0, starting transfers between devices: 16.6 us -> none  [the longest x1 11.9 us: shards(): lax.all_to_all(flat_act, ('expert', 'dp'), split_axis=0, concat_axis=0, t...]
    reshape x4 -> x2, local copies, waits for them, and re-layouts: 17.4 us -> 9.76 us  [the longest x1 8.11 us: shards(): recv_both = recv_both.reshape(buffer_rows, 2 * slice_width)]
  transfers between devices with their start and end apart: 4 -> 3, of which waited for: 4 -> 3; matrix products, arithmetic and copies ran while one was open for 11% -> 5% of each run, Pallas kernels for 0% -> 0%
where the time goes in v1:
time: 349 us; the launch traced here: 348 us
  waiting for transfers between devices  150 us (43%)
  blocking collectives  98.5 us (28%)
  matrix products  39.8 us (11%)
  local copies, waits for them, and re-layouts  25.7 us (7%)
  between operations  14.3 us (4%)
  other arithmetic  10.8 us (3%)
  starting transfers between devices  9.26 us (3%)
    all_to_all x1, blocking collectives, shards(): lax.all_to_all(flat_both, ('expert', 'dp'), split_axis=0, concat_axis=0,...  98.5 us
    reduce_scatter x1, waiting for transfers between devices, shards(): lax.psum_scatter(jnp.concatenate([gate_part, up_part, back_part], axis=1)...  72.4 us
    all_gather x1, waiting for transfers between devices, shards(): lax.all_gather(jnp.concatenate([grad_pre, grad_lin, activated], axis=1),...  45.8 us
    all_to_all x1, waiting for transfers between devices, shards(): lax.all_to_all(flat_back, ('expert', 'dp'), split_axis=0, concat_axis=0,...  31.4 us
    dot_general x5, matrix products, contract_rows(): lax.dot_general(left, right, (((0,), (0,)), ((), ())), preferred_element_...  20.5 us
    all_to_all x1, starting transfers between devices, shards(): lax.all_to_all(flat_back, ('expert', 'dp'), split_axis=0, concat_axis=0,...  9.18 us
    reshape x1, local copies, waits for them, and re-layouts, shards(): recv_both = recv_both.reshape(buffer_rows, 2 * slice_width)  8.11 us
  transfers between devices with their start and end apart: 3, of which 3 were waited for; matrix products, arithmetic and copies ran while one was open for 5% of the time, Pallas kernels for 0%

profile of v1, /device:TPU:1, one launch (start us, length us, event | category | flops | bytes accessed | tf_op | source)
XLA Modules:
  0.0 347.9 jit_solution(13178940153341892583)
XLA Ops:
  7.2 0.0 copy-start
  7.2 0.0 reduce-scatter.2.cloned.1.call-start
  7.2 0.8 copy.28
  8.0 0.1 eq.28
  8.1 0.1 fusion.29
  8.2 0.0 copy-start.3
  8.2 0.2 reduce_window_sum.11
  8.4 0.2 select_reduce_fusion.1
  8.6 0.1 reduce_sum.21
  8.7 0.1 fusion.28
  8.8 0.8 copy.30
  9.6 0.1 select_reduce_fusion
  9.7 0.0 copy-done
  9.7 2.2 fusion
  11.9 3.5 reshape.40
  15.4 0.0 copy-done.3
  15.4 2.2 convolution_convert_fusion
  17.6 4.6 %reshape.39 = bf16[32,5,4,1792]{3,2,1,0:T(4,128)(2,1)} reshape(bf16[160,7168]{1,0:T(8,128)(2,1)} %convolution_convert_fusion) | data formatting | bytes 4587520 | tf_op jit(solution)/shard_map/reshape | solution.py:45
  22.2 3.7 %maximum_bitcast_fusion = bf16[32,4,5,3584]{3,1,2,0:T(4,128)(2,1)S(1)} fusion(bf16[32,5,4,1792]{3,2,1,0:T(4,128)(2,1)S(1)} %reshape.40, bf16[32,5,4,1792]{3,2,1,0:T(4,128)(2,1)} %reshape.39), kind=kLoop, calls=%fused_computation.5 | loop fusion | flops 9175040 | bytes 9175040 | tf_op jit(solution)/shard_map/transpose | solution.py:48
  25.9 1.7 copy.36
  27.6 98.5 %all_to_all.10 = bf16[128,5,3584]{2,1,0:T(8,128)(2,1)} all-to-all(bf16[128,5,3584]{2,1,0:T(8,128)(2,1)S(1)} %bitcast.36), channel_id=1, replica_groups=mesh['expert'=32,'dp'=4] {'expert','dp'}, dimensions={0} | all-to-all | bytes 9175040 | tf_op jit(solution)/shard_map/all_to_all | solution.py:51
  126.1 8.1 %reshape.42 = bf16[640,3584]{1,0:T(8,128)(2,1)} reshape(bf16[128,5,3584]{2,1,0:T(8,128)(2,1)} %all_to_all.10) | data formatting | bytes 9175040 | tf_op jit(solution)/shard_map/reshape | solution.py:52
  134.2 5.4 %fusion.1 = f32[640,1024]{1,0:T(8,128)S(1)} fusion(bf16[1,1024,1792]{2,1,0:T(8,128)(2,1)} %param.13, bf16[640,3584]{1,0:T(8,128)(2,1)} %reshape.42), kind=kOutput, calls=%fused_computation.10 | convolution fusion | flops 2348810240 | bytes 8585216 | tf_op jit(solution)/shard_map/dot_general | solution.py:60
  139.7 0.0 copy-done.2
  139.7 0.0 copy-start.7
  139.7 2.5 fusion.5
  142.2 2.5 fusion.9
  144.8 3.4 pad_maximum_fusion
  148.2 0.0 reduce-scatter.2.cloned.1.call-update
  148.2 0.0 all-gather.2.cloned.1.call-start
  148.3 72.4 %reduce-scatter.2.cloned.1.call-done = f32[160,3072]{1,0:T(8,128)} async-done(((f32[640,3072]{1,0:T(8,128)}), f32[160,3072]{1,0:T(8,128)}) %reduce-scatter.2.cloned.1.call-update) | async-done | bytes 1966096 | tf_op jit(solution)/shard_map/reduce_scatter | solution.py:63
  220.7 1.9 multiply_convert_fusion.2
  222.6 1.0 pad_maximum_fusion.1
  223.6 0.0 all-gather.2.cloned.1.call-update
  223.7 45.8 %all-gather.2.cloned.1.call-done = bf16[640,3072]{1,0:T(8,128)(2,1)} async-done(((bf16[160,3072]{1,0:T(8,128)(2,1)}), bf16[640,3072]{1,0:T(8,128)(2,1)}) %all-gather.2.cloned.1.call-update) | async-done | bytes 3932176 | tf_op jit(solution)/shard_map/all_gather | solution.py:72
  269.4 5.2 %fusion.3 = f32[640,1792]{1,0:T(8,128)S(1)} fusion(bf16[1,1792,1024]{2,1,0:T(8,128)(2,1)} %param.12, bf16[640,3072]{1,0:T(8,128)(2,1)} %all-gather.2.cloned.1.call-done), kind=kOutput, calls=%fused_computation.12 | convolution fusion | flops 2348810240 | bytes 9568256 | tf_op jit(solution)/shard_map/dot_general | solution.py:80
  274.6 2.6 add_convert_fusion
  277.2 2.7 reshape.43
  279.9 9.2 %all-to-all-start.1 = ((bf16[128,5,1792]{2,1,0:T(8,128)(2,1)}), bf16[128,5,1792]{2,1,0:T(8,128)(2,1)}, u32[]{:S(2)}, u32[]{:S(2)}) async-start(bf16[128,5,1792]{2,1,0:T(8,128)(2,1)} %reshape.43), calls=%async_computation.2 | async-start | bytes 7340032 | tf_op jit(solution)/shard_map/all_to_all | solution.py:88
  289.1 0.0 slice-start.1
  289.1 7.1 %fusion.11 = bf16[1,1792,1024]{2,1,0:T(8,128)(2,1)} fusion(bf16[640,3584]{1,0:T(8,128)(2,1)} %reshape.42, bf16[640,3072]{1,0:T(8,128)(2,1)} %all-gather.2.cloned.1.call-done), kind=kOutput, calls=%fused_computation.20 | convolution fusion | flops 2350645248 | bytes 7274496 | tf_op jit(solution)/shard_map/dot_general | solution.py:17
  296.2 0.0 slice-done
  296.2 4.5 %fusion.12 = bf16[1,1792,1024]{2,1,0:T(8,128)(2,1)} fusion(bf16[640,3584]{1,0:T(8,128)(2,1)S(1)} %bitcast.40, bf16[640,3072]{1,0:T(8,128)(2,1)S(1)} %copy-done.5), kind=kOutput, calls=%fused_computation.21 | convolution fusion | flops 2350645248 | bytes 7274496 | tf_op jit(solution)/shard_map/dot_general | solution.py:17
  300.8 4.5 %fusion.13 = bf16[1,1024,1792]{2,1,0:T(8,128)(2,1)} fusion(bf16[640,3584]{1,0:T(8,128)(2,1)S(1)} %bitcast.40, bf16[640,3072]{1,0:T(8,128)(2,1)S(1)} %copy-done.5), kind=kOutput, calls=%fused_computation.22 | convolution fusion | flops 2350645248 | bytes 7274496 | tf_op jit(solution)/shard_map/dot_general | solution.py:17
  305.3 31.4 %all-to-all-done.1 = bf16[128,5,1792]{2,1,0:T(8,128)(2,1)} async-done(((bf16[128,5,1792]{2,1,0:T(8,128)(2,1)}), bf16[128,5,1792]{2,1,0:T(8,128)(2,1)}, u32[]{:S(2)}, u32[]{:S(2)}) %all-to-all-start.1) | async-done | bytes 2293792 | tf_op jit(solution)/shard_map/all_to_all | solution.py:88
  336.6 3.0 copy.34
  339.7 0.3 copy.38
  340.0 1.1 convolution_convert_fusion.1
  (16 shorter events, 0.0 us)
Async XLA Ops:
  7.2 2.5 copy-start
  7.2 213.5 %reduce-scatter.2.cloned.1.call-start = ((), (), s32[]{:S(2)}) async-start(), calls=%async_computation.3 | async-start | bytes 9830400 | tf_op jit(solution)/shard_map/reduce_scatter | solution.py:63
  8.2 7.2 %copy-start.3 = (bf16[16,7168]{1,0:T(8,128)(2,1)S(1)}, bf16[16,7168]{1,0:T(8,128)(2,1)}, u32[]{:S(2)}) copy-start(bf16[16,7168]{1,0:T(8,128)(2,1)} %param.7) | copy-start | bytes 688132
  134.2 5.4 %copy-start.2 = (bf16[640,3584]{1,0:T(8,128)(2,1)S(1)}, bf16[640,3584]{1,0:T(8,128)(2,1)}, u32[]{:S(2)}) copy-start(bf16[640,3584]{1,0:T(8,128)(2,1)} %reshape.42) | copy-start | bytes 13762564
  134.2 5.5 %copy-start.6 = (bf16[1,1792,1024]{2,1,0:T(8,128)(2,1)S(1)}, bf16[1,1792,1024]{2,1,0:T(8,128)(2,1)}, u32[]{:S(2)}) copy-start(bf16[1,1792,1024]{2,1,0:T(8,128)(2,1)} %param.12) | copy-start | bytes 11010052
  139.7 2.5 copy-start.7
  148.2 121.2 %all-gather.2.cloned.1.call-start = ((), (), s32[]{:S(2)}) async-start(), calls=%async_computation.4 | async-start | bytes 4915200 | tf_op jit(solution)/shard_map/all_gather | solution.py:72
  269.4 5.2 %copy-start.4 = (bf16[640,3072]{1,0:T(8,128)(2,1)S(1)}, bf16[640,3072]{1,0:T(8,128)(2,1)}, u32[]{:S(2)}) copy-start(bf16[640,3072]{1,0:T(8,128)(2,1)} %all-gather.2.cloned.1.call-done) | copy-start | bytes 11796484
  269.4 5.2 %copy-start.8 = (bf16[1,1792,1024]{2,1,0:T(8,128)(2,1)S(1)}, bf16[1,1792,1024]{2,1,0:T(8,128)(2,1)}, u32[]{:S(2)}) copy-start(bf16[1,1792,1024]{2,1,0:T(8,128)(2,1)} %param.11) | copy-start | bytes 11010052
  279.9 16.3 %slice-start = ((s8[4587520]{0:T(1024)(128)(4,1)}), s8[393216]{0:T(1024)(128)(4,1)S(1)}, s32[]{:S(2)}) async-start(s8[4587520]{0:T(1024)(128)(4,1)} %bitcast.39), calls=%async_computation.5 | async-start | bytes 786432
  279.9 56.7 %all-to-all-start.1 = ((bf16[128,5,1792]{2,1,0:T(8,128)(2,1)}), bf16[128,5,1792]{2,1,0:T(8,128)(2,1)}, u32[]{:S(2)}, u32[]{:S(2)}) async-start(bf16[128,5,1792]{2,1,0:T(8,128)(2,1)} %reshape.43), calls=%async_computation.2 | async-start | bytes 7340032 | tf_op jit(solution)/shard_map/all_to_all | solution.py:88
  289.1 7.1 %slice-start.1 = ((s8[4587520]{0:T(1024)(128)(4,1)}), s8[4194304]{0:T(1024)(128)(4,1)S(1)}, s32[]{:S(2)}) async-start(s8[4587520]{0:T(1024)(128)(4,1)} %bitcast.39), calls=%async_computation.6 | async-start | bytes 8388608
  289.1 7.1 %copy-start.5 = (bf16[640,3072]{1,0:T(8,128)(2,1)S(1)}, bf16[640,3072]{1,0:T(8,128)(2,1)}, u32[]{:S(2)}) copy-start(bf16[640,3072]{1,0:T(8,128)(2,1)} %all-gather.2.cloned.1.call-done) | copy-start | bytes 11796484
  336.6 4.5 %copy-start.1 = (bf16[16,7168]{1,0:T(8,128)(2,1)S(1)}, bf16[16,7168]{1,0:T(8,128)(2,1)}, u32[]{:S(2)}) copy-start(bf16[16,7168]{1,0:T(8,128)(2,1)} %param.8) | copy-start | bytes 688132
Sparse Core Ops, SparseCore 0:
  148.3 72.2 reduce-scatter.1
  223.8 45.6 all-gather.1

commit v2 on v1

--- a/solution.py
+++ b/solution.py
@@ -60,12 +60,16 @@
     back_part = lax.dot_general(
         cot_rows, down_local, (((1,), (1,)), ((), ())), preferred_element_type=jnp.float32
     )
-    summed = lax.psum_scatter(
-        jnp.concatenate([gate_part, up_part, back_part], axis=1),
-        "dp",
-        scatter_dimension=0,
-        tiled=True,
+    parts = jnp.concatenate([gate_part, up_part, back_part], axis=1)
+    quarter = buffer_rows // num_dp
+    parts = parts.reshape(num_dp, quarter, 3 * hidden)
+    me = lax.axis_index("dp")
+    own = lax.dynamic_index_in_dim(parts, me, 0, keepdims=False)
+    came = lax.all_to_all(
+        parts.astype(jnp.bfloat16), "dp", split_axis=0, concat_axis=0, tiled=True
     )
+    others = (jnp.arange(num_dp, dtype=jnp.int32) != me).astype(jnp.float32)
+    summed = own + jnp.sum(came.astype(jnp.float32) * others[:, None, None], axis=0)
     grad_pre, grad_lin, activated = swiglu_back(
         summed[:, :hidden], summed[:, hidden : 2 * hidden], summed[:, 2 * hidden :]
     )

time: 349 us -> 329 us (0.943)
  waiting for transfers between devices: 150 us -> 119 us
  starting transfers between devices: 9.26 us -> 14.1 us
    reduce_scatter x1 -> x0, waiting for transfers between devices: 72.4 us -> none  [shards(): lax.psum_scatter(jnp.concatenate([gate_part, up_part, back_part], axis=1)...]
    all_to_all x0 -> x1, waiting for transfers between devices: none -> 45.9 us  [shards(): lax.all_to_all(parts.astype(jnp.bfloat16), 'dp', split_axis=0, concat_axi...]
    all_to_all x0 -> x1, starting transfers between devices: none -> 4.86 us  [shards(): lax.all_to_all(parts.astype(jnp.bfloat16), 'dp', split_axis=0, concat_axi...]
    all_gather x1, waiting for transfers between devices: 45.8 us -> 41.4 us  [shards(): lax.all_gather(jnp.concatenate([grad_pre, grad_lin, activated], axis=1),...]
where the time goes in v2:
time: 329 us; the launch traced here: 328 us
  waiting for transfers between devices  119 us (36%)
  blocking collectives  98.5 us (30%)
  matrix products  39.8 us (12%)
  local copies, waits for them, and re-layouts  28.8 us (9%)
  between operations  14.3 us (4%)
  other arithmetic  14.1 us (4%)
  starting transfers between devices  14.1 us (4%)
    all_to_all x1, blocking collectives, shards(): lax.all_to_all(flat_both, ('expert', 'dp'), split_axis=0, concat_axis=0,...  98.5 us
    all_to_all x1, waiting for transfers between devices, shards(): lax.all_to_all(parts.astype(jnp.bfloat16), 'dp', split_axis=0, concat_axi...  45.9 us
    all_gather x1, waiting for transfers between devices, shards(): lax.all_gather(jnp.concatenate([grad_pre, grad_lin, activated], axis=1),...  41.4 us
    all_to_all x1, waiting for transfers between devices, shards(): lax.all_to_all(flat_back, ('expert', 'dp'), split_axis=0, concat_axis=0,...  31.4 us
    dot_general x5, matrix products, contract_rows(): lax.dot_general(left, right, (((0,), (0,)), ((), ())), preferred_element_...  20.5 us
    all_to_all x1, starting transfers between devices, shards(): lax.all_to_all(flat_back, ('expert', 'dp'), split_axis=0, concat_axis=0,...  9.17 us
    reshape x1, local copies, waits for them, and re-layouts, shards(): recv_both = recv_both.reshape(buffer_rows, 2 * slice_width)  8.11 us
  transfers between devices with their start and end apart: 3, of which 3 were waited for; matrix products, arithmetic and copies ran while one was open for 5% of the time, Pallas kernels for 0%

profile of v2, /device:TPU:1, one launch (start us, length us, event | category | flops | bytes accessed | tf_op | source)
XLA Modules:
  0.0 328.2 jit_solution(9575912663250071960)
XLA Ops:
  7.2 0.0 copy-start
  7.2 0.8 copy.28
  8.0 0.1 eq.28
  8.1 0.1 fusion.29
  8.2 0.0 copy-start.4
  8.2 0.2 reduce_window_sum.11
  8.4 0.2 select_reduce_fusion.1
  8.5 0.1 reduce_sum.30
  8.6 0.1 fusion.28
  8.8 0.8 copy.30
  9.5 0.1 select_reduce_fusion
  9.7 2.2 fusion
  11.8 3.5 %reshape.48 = bf16[32,5,4,1792]{3,2,1,0:T(4,128)(2,1)S(1)} reshape(bf16[160,7168]{1,0:T(8,128)(2,1)} %fusion) | data formatting | bytes 4587520 | tf_op jit(solution)/shard_map/reshape | solution.py:46
  15.3 0.0 copy-done.4
  15.3 2.2 convolution_convert_fusion
  17.5 4.6 %reshape.47 = bf16[32,5,4,1792]{3,2,1,0:T(4,128)(2,1)} reshape(bf16[160,7168]{1,0:T(8,128)(2,1)} %convolution_convert_fusion) | data formatting | bytes 4587520 | tf_op jit(solution)/shard_map/reshape | solution.py:45
  22.1 3.7 %maximum_bitcast_fusion = bf16[32,4,5,3584]{3,1,2,0:T(4,128)(2,1)S(1)} fusion(bf16[32,5,4,1792]{3,2,1,0:T(4,128)(2,1)S(1)} %reshape.48, bf16[32,5,4,1792]{3,2,1,0:T(4,128)(2,1)} %reshape.47), kind=kLoop, calls=%fused_computation.6 | loop fusion | flops 9175040 | bytes 9175040 | tf_op jit(solution)/shard_map/transpose | solution.py:48
  25.9 1.7 copy.36
  27.5 98.5 %all_to_all.15 = bf16[128,5,3584]{2,1,0:T(8,128)(2,1)} all-to-all(bf16[128,5,3584]{2,1,0:T(8,128)(2,1)S(1)} %bitcast.41), channel_id=1, replica_groups=mesh['expert'=32,'dp'=4] {'expert','dp'}, dimensions={0} | all-to-all | bytes 9175040 | tf_op jit(solution)/shard_map/all_to_all | solution.py:51
  126.1 8.1 %reshape.50 = bf16[640,3584]{1,0:T(8,128)(2,1)} reshape(bf16[128,5,3584]{2,1,0:T(8,128)(2,1)} %all_to_all.15) | data formatting | bytes 9175040 | tf_op jit(solution)/shard_map/reshape | solution.py:52
  134.2 5.4 %fusion.1 = f32[640,1024]{1,0:T(8,128)S(1)} fusion(bf16[1,1024,1792]{2,1,0:T(8,128)(2,1)} %param.13, bf16[640,3584]{1,0:T(8,128)(2,1)} %reshape.50), kind=kOutput, calls=%fused_computation.11 | convolution fusion | flops 2348810240 | bytes 8585216 | tf_op jit(solution)/shard_map/dot_general | solution.py:60
  139.6 0.0 copy-start.8
  139.6 2.5 fusion.5
  142.2 2.5 fusion.9
  144.7 0.6 pad_maximum_fusion
  145.4 3.0 copy-done.2
  148.4 2.5 convert_element_type.50
  150.9 4.9 %all-to-all-start.1 = ((bf16[4,160,3072]{2,1,0:T(8,128)(2,1)}), bf16[4,160,3072]{2,1,0:T(8,128)(2,1)}, u32[]{:S(2)}, u32[]{:S(2)}) async-start(bf16[4,160,3072]{2,1,0:T(8,128)(2,1)} %convert_element_type.50), calls=%async_computation.1 | async-start | bytes 7864320 | tf_op jit(solution)/shard_map/all_to_all | solution.py:68
  155.7 0.0 all-gather.2.cloned.1.call-start
  155.8 45.9 %all-to-all-done.1 = bf16[4,160,3072]{2,1,0:T(8,128)(2,1)} async-done(((bf16[4,160,3072]{2,1,0:T(8,128)(2,1)}), bf16[4,160,3072]{2,1,0:T(8,128)(2,1)}, u32[]{:S(2)}, u32[]{:S(2)}) %all-to-all-start.1) | async-done | bytes 3932192 | tf_op jit(solution)/shard_map/all_to_all | solution.py:68
  201.7 3.3 multiply_reduce_fusion
  205.0 1.9 bitcast_add_fusion
  206.9 0.4 multiply_convert_fusion.2
  207.3 1.0 pad_maximum_fusion.1
  208.3 0.0 all-gather.2.cloned.1.call-update
  208.3 41.4 %all-gather.2.cloned.1.call-done = bf16[640,3072]{1,0:T(8,128)(2,1)} async-done(((bf16[160,3072]{1,0:T(8,128)(2,1)}), bf16[640,3072]{1,0:T(8,128)(2,1)}) %all-gather.2.cloned.1.call-update) | async-done | bytes 3932176 | tf_op jit(solution)/shard_map/all_gather | solution.py:76
  249.7 5.2 %fusion.3 = f32[640,1792]{1,0:T(8,128)S(1)} fusion(bf16[1,1792,1024]{2,1,0:T(8,128)(2,1)} %param.12, bf16[640,3072]{1,0:T(8,128)(2,1)} %all-gather.2.cloned.1.call-done), kind=kOutput, calls=%fused_computation.13 | convolution fusion | flops 2348810240 | bytes 9568256 | tf_op jit(solution)/shard_map/dot_general | solution.py:84
  254.9 2.6 add_convert_fusion
  257.5 2.7 reshape.52
  260.2 9.2 %all-to-all-start.2 = ((bf16[128,5,1792]{2,1,0:T(8,128)(2,1)}), bf16[128,5,1792]{2,1,0:T(8,128)(2,1)}, u32[]{:S(2)}, u32[]{:S(2)}) async-start(bf16[128,5,1792]{2,1,0:T(8,128)(2,1)} %reshape.52), calls=%async_computation.2 | async-start | bytes 7340032 | tf_op jit(solution)/shard_map/all_to_all | solution.py:92
  269.4 0.0 slice-start.1
  269.4 7.1 %fusion.11 = bf16[1,1792,1024]{2,1,0:T(8,128)(2,1)} fusion(bf16[640,3584]{1,0:T(8,128)(2,1)} %reshape.50, bf16[640,3072]{1,0:T(8,128)(2,1)} %all-gather.2.cloned.1.call-done), kind=kOutput, calls=%fused_computation.21 | convolution fusion | flops 2350645248 | bytes 7274496 | tf_op jit(solution)/shard_map/dot_general | solution.py:17
  276.5 4.5 %fusion.12 = bf16[1,1792,1024]{2,1,0:T(8,128)(2,1)} fusion(bf16[640,3584]{1,0:T(8,128)(2,1)S(1)} %bitcast.45, bf16[640,3072]{1,0:T(8,128)(2,1)S(1)} %copy-done.6), kind=kOutput, calls=%fused_computation.22 | convolution fusion | flops 2350645248 | bytes 7274496 | tf_op jit(solution)/shard_map/dot_general | solution.py:17
  281.0 4.5 %fusion.13 = bf16[1,1024,1792]{2,1,0:T(8,128)(2,1)} fusion(bf16[640,3584]{1,0:T(8,128)(2,1)S(1)} %bitcast.45, bf16[640,3072]{1,0:T(8,128)(2,1)S(1)} %copy-done.6), kind=kOutput, calls=%fused_computation.23 | convolution fusion | flops 2350645248 | bytes 7274496 | tf_op jit(solution)/shard_map/dot_general | solution.py:17
  285.5 31.4 %all-to-all-done.2 = bf16[128,5,1792]{2,1,0:T(8,128)(2,1)} async-done(((bf16[128,5,1792]{2,1,0:T(8,128)(2,1)}), bf16[128,5,1792]{2,1,0:T(8,128)(2,1)}, u32[]{:S(2)}, u32[]{:S(2)}) %all-to-all-start.2) | async-done | bytes 2293792 | tf_op jit(solution)/shard_map/all_to_all | solution.py:92
  316.9 3.0 copy.34
  320.0 0.3 copy.38
  320.3 1.1 convolution_convert_fusion.1
  (21 shorter events, 0.1 us)
Async XLA Ops:
  7.2 2.5 copy-start
  8.2 7.2 %copy-start.4 = (bf16[16,7168]{1,0:T(8,128)(2,1)S(1)}, bf16[16,7168]{1,0:T(8,128)(2,1)}, u32[]{:S(2)}) copy-start(bf16[16,7168]{1,0:T(8,128)(2,1)} %param.7) | copy-start | bytes 688132
  134.2 5.4 %copy-start.3 = (bf16[640,3584]{1,0:T(8,128)(2,1)S(1)}, bf16[640,3584]{1,0:T(8,128)(2,1)}, u32[]{:S(2)}) copy-start(bf16[640,3584]{1,0:T(8,128)(2,1)} %reshape.50) | copy-start | bytes 13762564
  134.2 5.5 %copy-start.7 = (bf16[1,1792,1024]{2,1,0:T(8,128)(2,1)S(1)}, bf16[1,1792,1024]{2,1,0:T(8,128)(2,1)}, u32[]{:S(2)}) copy-start(bf16[1,1792,1024]{2,1,0:T(8,128)(2,1)} %param.12) | copy-start | bytes 11010052
  139.6 2.5 copy-start.8
  145.4 3.1 copy-start.2
  150.9 50.9 %all-to-all-start.1 = ((bf16[4,160,3072]{2,1,0:T(8,128)(2,1)}), bf16[4,160,3072]{2,1,0:T(8,128)(2,1)}, u32[]{:S(2)}, u32[]{:S(2)}) async-start(bf16[4,160,3072]{2,1,0:T(8,128)(2,1)} %convert_element_type.50), calls=%async_computation.1 | async-start | bytes 7864320 | tf_op jit(solution)/shard_map/all_to_all | solution.py:68
  155.7 94.0 %all-gather.2.cloned.1.call-start = ((), (), s32[]{:S(2)}) async-start(), calls=%async_computation.3 | async-start | bytes 4915200 | tf_op jit(solution)/shard_map/all_gather | solution.py:76
  249.7 5.2 %copy-start.5 = (bf16[640,3072]{1,0:T(8,128)(2,1)S(1)}, bf16[640,3072]{1,0:T(8,128)(2,1)}, u32[]{:S(2)}) copy-start(bf16[640,3072]{1,0:T(8,128)(2,1)} %all-gather.2.cloned.1.call-done) | copy-start | bytes 11796484
  249.7 5.2 %copy-start.9 = (bf16[1,1792,1024]{2,1,0:T(8,128)(2,1)S(1)}, bf16[1,1792,1024]{2,1,0:T(8,128)(2,1)}, u32[]{:S(2)}) copy-start(bf16[1,1792,1024]{2,1,0:T(8,128)(2,1)} %param.11) | copy-start | bytes 11010052
  260.2 16.3 %slice-start = ((s8[4587520]{0:T(1024)(128)(4,1)}), s8[393216]{0:T(1024)(128)(4,1)S(1)}, s32[]{:S(2)}) async-start(s8[4587520]{0:T(1024)(128)(4,1)} %bitcast.44), calls=%async_computation.4 | async-start | bytes 786432
  260.2 56.7 %all-to-all-start.2 = ((bf16[128,5,1792]{2,1,0:T(8,128)(2,1)}), bf16[128,5,1792]{2,1,0:T(8,128)(2,1)}, u32[]{:S(2)}, u32[]{:S(2)}) async-start(bf16[128,5,1792]{2,1,0:T(8,128)(2,1)} %reshape.52), calls=%async_computation.2 | async-start | bytes 7340032 | tf_op jit(solution)/shard_map/all_to_all | solution.py:92
  269.4 7.1 %slice-start.1 = ((s8[4587520]{0:T(1024)(128)(4,1)}), s8[4194304]{0:T(1024)(128)(4,1)S(1)}, s32[]{:S(2)}) async-start(s8[4587520]{0:T(1024)(128)(4,1)} %bitcast.44), calls=%async_computation.5 | async-start | bytes 8388608
  269.4 7.1 %copy-start.6 = (bf16[640,3072]{1,0:T(8,128)(2,1)S(1)}, bf16[640,3072]{1,0:T(8,128)(2,1)}, u32[]{:S(2)}) copy-start(bf16[640,3072]{1,0:T(8,128)(2,1)} %all-gather.2.cloned.1.call-done) | copy-start | bytes 11796484
  316.9 4.5 %copy-start.1 = (bf16[16,7168]{1,0:T(8,128)(2,1)S(1)}, bf16[16,7168]{1,0:T(8,128)(2,1)}, u32[]{:S(2)}) copy-start(bf16[16,7168]{1,0:T(8,128)(2,1)} %param.8) | copy-start | bytes 688132
Sparse Core Ops, SparseCore 0:
  208.5 41.1 all-gather.1
